TPU v7x, 32 devices: a whole 2x2x4 slice. The times are simulated.
32 devices in a mesh: section: 4 (over y, x), tp: 4 (over z), mirror: 2 (over core).
Axes of the slice: x: 2, y: 2, z: 4, core: 2. Of those that a mesh axis runs over, the one named last changes fastest.
Arguments:
- feats: bfloat16 [2, 2, 128, 5120], P('mirror', None, 'tp'), may hold values from -16 to 16
- types: int32 [2, 2, 128], P('mirror', None, 'tp'), may hold values from 0 to 63
- segs: int32 [2, 2, 5, 128], P('mirror'), may hold values from 0 to 3, never falling along the last dimension, each value on 1 to 64 neighbouring positions
- type_table: bfloat16 [64, 5120], replicated, may hold values from -3 to 3
- gains: float32 [2, 4, 5120], P('mirror', 'section'), may hold values from 0.25 to 1.75, as said below
- w_qkv: bfloat16 [2, 4, 3, 5120, 512], P('mirror', 'section', None, None, 'tp'), may hold values from -8 to 8, as said below
- w_out: bfloat16 [2, 4, 512, 5120], P('mirror', 'section', 'tp'), as said below
- carry_acts: bfloat16 [2, 4, 128, 5120], P('mirror', 'section', 'tp'), may hold values from -16 to 16
- grad_in: bfloat16 [2, 4, 128, 5120], P('mirror', 'section', 'tp'), may hold values from -6 to 6
- saved: bfloat16 [2, 4, 2, 128, 5120], P('mirror', 'section', None, 'tp'), may hold values from -16 to 16
- cotangent: bfloat16 [2, 2, 128, 5120], P('mirror', None, 'tp'), may hold values from -6 to 6
Outputs:
- acts: bfloat16 [2, 4, 2, 128, 5120], P('mirror', 'section', None, 'tp')
- grad_acts: bfloat16 [2, 4, 2, 128, 5120], P('mirror', 'section', None, 'tp')
- grad_qkv: bfloat16 [2, 4, 3, 5120, 512], P('mirror', 'section', None, None, 'tp')
- grad_out: bfloat16 [2, 4, 512, 5120], P('mirror', 'section', 'tp')
Inputs may be any that keep to these rules, and one draw needn't show every extreme that they name: w_qkv[1, k] equals w_qkv[0, 3 - k]. w_out[1, k] equals w_out[0, 3 - k]. gains[1, k] equals gains[0, 3 - k]. `segs`: segment numbers never fall along a micro-batch; each segment holds at most half of 128 tokens, and one holds exactly that many.
All inputs are finite; a program needn't handle non-finite values.
Results may differ from a plain program's by a relative error of at most 0.015.
Values may be sent and summed in bfloat16 or wider, within the bound.
No kernel may reach another device: no remote copies, remote signals or barrier semaphores. Data moves between devices by JAX's collectives and lax.ppermute only.
A program may use at most 128 MiB of HBM per device.

v0:
```python
import math
import jax
import jax.numpy as jnp
from jax import lax
from jax.sharding import PartitionSpec as P

HD = 128


def passed_along(block, axis, distance):
    devices = range(lax.axis_size(axis))
    route = [(i - distance, i) for i in devices if i - distance in devices]
    return lax.ppermute(block, axis, route)


def swapped(value, axis, apart):
    return lax.ppermute(value, axis, [(i, i ^ 1 << apart) for i in range(lax.axis_size(axis))])


def normalize(values, gain_row):
    mean_square = jnp.mean(values * values, axis=-1, keepdims=True)
    return values * lax.rsqrt(mean_square + 1e-05) * gain_row


def segment_mask(segment_ids):
    position = jnp.arange(segment_ids.shape[0], dtype=jnp.int32)
    causal = position[None, :] <= position[:, None]
    return causal & (segment_ids[:, None] == segment_ids[None, :])


def attend(queries, keys_all, values_all, seg_mask):
    scores = jnp.einsum(
        "ihd,jhd->hij", queries, keys_all, preferred_element_type=jnp.float32
    ) / math.sqrt(queries.shape[-1])
    scores = jnp.where(seg_mask[None], scores, -1e30)
    highest = lax.stop_gradient(jnp.max(scores, axis=-1, keepdims=True))
    expo = jnp.exp(scores - highest)
    probs = (expo / jnp.sum(expo, axis=-1, keepdims=True)).astype(values_all.dtype)
    return jnp.einsum("hij,jhd->ihd", probs, values_all, preferred_element_type=jnp.float32)


def embedding(feat_rows, type_rows, type_table):
    onehot = (
        type_rows[:, None] == jnp.arange(type_table.shape[0], dtype=jnp.int32)[None, :]
    ).astype(jnp.bfloat16)
    looked = jnp.dot(onehot, type_table, preferred_element_type=jnp.float32)
    return (feat_rows.astype(jnp.float32) + looked).astype(jnp.bfloat16)


def shards(
    feats, types, segs, type_table, gains, w_qkv, w_out, carry_acts, grad_in, saved, cotangent
):
    sections = lax.axis_size("section")
    section_index = lax.axis_index("section")
    on_first_pipe = lax.axis_index("mirror") == 0
    position = jnp.where(on_first_pipe, section_index, sections - 1 - section_index)
    gain_row = gains[0, 0]
    qkv_weight = w_qkv[0, 0]
    out_weight = w_out[0, 0]
    window_steps = feats.shape[1]
    seq_len = segs.shape[3]
    model_width = qkv_weight.shape[1]
    inner_here = qkv_weight.shape[-1]
    heads_here = inner_here // HD

    def mask_for(which, index):
        return segment_mask(lax.dynamic_index_in_dim(segs[0, which], index, 0, keepdims=False))

    def backward_layer(layer_in, upstream, seg_mask):
        normed = normalize(layer_in.astype(jnp.float32), gain_row).astype(jnp.bfloat16)
        normed_full, upstream_full = (
            lax.all_gather(normed, "tp", axis=0, tiled=True),
            lax.all_gather(upstream, "tp", axis=0, tiled=True),
        )
        projected = jnp.einsum(
            "sd,cdn->csn", normed_full, qkv_weight, preferred_element_type=jnp.float32
        ).astype(jnp.bfloat16)
        heads_view = projected.reshape(3, seq_len, heads_here, HD)
        primal, pull_attend = jax.vjp(
            lambda query_part, key_part, value_part: attend(
                query_part, key_part, value_part, seg_mask
            ),
            heads_view[0],
            heads_view[1],
            heads_view[2],
        )
        mixed = primal.reshape(seq_len, inner_here).astype(jnp.bfloat16)
        d_mixed = jnp.einsum(
            "sd,nd->sn", upstream_full, out_weight, preferred_element_type=jnp.float32
        ).astype(jnp.bfloat16)
        pulled = pull_attend(d_mixed.astype(jnp.float32).reshape(seq_len, heads_here, HD))
        d_projected = jnp.stack(pulled).reshape(3, seq_len, inner_here)
        d_normed = lax.psum_scatter(
            jnp.einsum(
                "csn,cdn->sd", d_projected, qkv_weight, preferred_element_type=jnp.float32
            ).astype(jnp.bfloat16),
            "tp",
            scatter_dimension=0,
            tiled=True,
        )
        unused_norm, pull_norm = jax.vjp(
            lambda inputs: normalize(inputs, gain_row), layer_in.astype(jnp.float32)
        )
        d_input = pull_norm(d_normed.astype(jnp.float32))[0]
        result = (upstream.astype(jnp.float32) + d_input).astype(jnp.bfloat16)
        qkv_term = jnp.einsum(
            "sd,csn->cdn", normed_full, d_projected, preferred_element_type=jnp.float32
        )
        out_term = jnp.einsum("sn,sd->nd", mixed, upstream_full, preferred_element_type=jnp.float32)
        return (result, qkv_term, out_term)

    forward_in = carry_acts[0, 0]
    backward_in = grad_in[0, 0]
    forward_outs = []
    backward_outs = []
    qkv_total = jnp.zeros(qkv_weight.shape, jnp.float32)
    out_total = jnp.zeros(out_weight.shape, jnp.float32)
    for step_index in range(window_steps):
        embedded = embedding(feats[0, step_index], types[0, step_index], type_table)
        current = jnp.where(position == 0, embedded, forward_in)
        forward_normed = normalize(current.astype(jnp.float32), gain_row).astype(jnp.bfloat16)
        forward_normed_full = lax.all_gather(forward_normed, "tp", axis=0, tiled=True)
        forward_projected = jnp.einsum(
            "sd,cdn->csn", forward_normed_full, qkv_weight, preferred_element_type=jnp.float32
        ).astype(jnp.bfloat16)
        forward_heads_view = forward_projected.reshape(3, seq_len, heads_here, HD)
        forward_mixed = (
            attend(
                forward_heads_view[0],
                forward_heads_view[1],
                forward_heads_view[2],
                mask_for(0, step_index - position + sections - 1),
            )
            .reshape(seq_len, inner_here)
            .astype(jnp.bfloat16)
        )
        attn_rows = lax.psum_scatter(
            jnp.dot(forward_mixed, out_weight, preferred_element_type=jnp.float32).astype(
                jnp.bfloat16
            ),
            "tp",
            scatter_dimension=0,
            tiled=True,
        ).astype(jnp.float32)
        forward_out = (current.astype(jnp.float32) + attn_rows).astype(jnp.bfloat16)
        upstream = jnp.where(position == sections - 1, cotangent[0, step_index], backward_in)
        backward_out, qkv_term, out_term = backward_layer(
            saved[0, 0, step_index], upstream, mask_for(1, step_index + position)
        )
        qkv_total = qkv_total + qkv_term
        out_total = out_total + out_term
        forward_outs.append(forward_out)
        backward_outs.append(backward_out)
        if step_index + 1 < window_steps:
            toward_higher = jnp.where(on_first_pipe, forward_out, backward_out)
            toward_lower = jnp.where(on_first_pipe, backward_out, forward_out)
            from_lower = passed_along(toward_higher, "section", 1)
            from_upper = passed_along(toward_lower, "section", -1)
            forward_in = jnp.where(on_first_pipe, from_lower, from_upper)
            backward_in = jnp.where(on_first_pipe, from_upper, from_lower)
    qkv_size = qkv_total.size
    own_terms = jnp.concatenate(
        [qkv_total.astype(jnp.bfloat16).reshape(-1), out_total.astype(jnp.bfloat16).reshape(-1)]
    )
    bit_count = lax.axis_size(("section", "mirror")).bit_length() - 1
    partner = own_terms
    for bit_number in range(bit_count):
        partner = swapped(partner, ("section", "mirror"), bit_number)
    summed = (own_terms.astype(jnp.float32) + partner.astype(jnp.float32)).astype(jnp.bfloat16)
    grad_qkv = summed[:qkv_size].reshape(3, model_width, inner_here)
    grad_out = summed[qkv_size:].reshape(inner_here, model_width)
    acts_block = jnp.stack(forward_outs)[None, None]
    grads_block = jnp.stack(backward_outs)[None, None]
    return (acts_block, grads_block, grad_qkv[None, None], grad_out[None, None])


def solution(mesh):
    in_specs = (
        P("mirror", None, "tp", None),
        P("mirror", None, "tp"),
        P("mirror", None, None, None),
        P(),
        P("mirror", "section", None),
        P("mirror", "section", None, None, "tp"),
        P("mirror", "section", "tp", None),
        P("mirror", "section", "tp", None),
        P("mirror", "section", "tp", None),
        P("mirror", "section", None, "tp", None),
        P("mirror", None, "tp", None),
    )
    out_specs = (
        P("mirror", "section", None, "tp", None),
        P("mirror", "section", None, "tp", None),
        P("mirror", "section", None, None, "tp"),
        P("mirror", "section", "tp", None),
    )
    return jax.shard_map(shards, mesh=mesh, in_specs=in_specs, out_specs=out_specs, check_vma=False)
```

profile of v0, /device:TPU:0, one launch (start us, length us, event | category | flops | bytes accessed | tf_op | source)
XLA Modules:
  0.0 553.4 jit_solution(733608073758702413)
XLA Ops:
  7.3 1.3 fusion.115
  8.6 1.9 fusion.117
  11.4 34.4 %all-gather.10.cloned.1.call-done = bf16[128,5120]{1,0:T(8,128)(2,1)} async-done(((bf16[32,5120]{1,0:T(8,128)(2,1)}), bf16[128,5120]{1,0:T(8,128)(2,1)}) %all-gather.10.cloned.1.call-update) | async-done | bytes 1310736 | tf_op jit(solution)/shard_map/all_gather | solution.py:72
  45.8 3.4 fusion.65
  49.4 30.3 %all-gather.18.cloned.1.call-done = bf16[1,1,128,5120]{3,2,1,0:T(8,128)(2,1)} async-done(((bf16[1,1,32,5120]{3,2,1,0:T(8,128)(2,1)}), bf16[1,1,128,5120]{3,2,1,0:T(8,128)(2,1)}) %all-gather.18.cloned.1.call-update) | async-done | bytes 1310736 | tf_op jit(solution)/shard_map/all_gather | solution.py:73
  79.7 1.8 fusion.99
  82.3 4.5 fusion.2
  88.0 2.0 multiply_reduce_fusion
  90.1 27.4 %reduce-scatter.7.cloned.1.call-done = bf16[32,5120]{1,0:T(8,128)(2,1)} async-done(((bf16[128,5120]{1,0:T(8,128)(2,1)}), bf16[32,5120]{1,0:T(8,128)(2,1)}) %reduce-scatter.7.cloned.1.call-update) | async-done | bytes 327696 | tf_op jit(solution)/shard_map/reduce_scatter | solution.py:93
  117.5 1.8 fusion.119
  121.6 30.7 %all-gather.8.cloned.1.call-done = bf16[128,5120]{1,0:T(8,128)(2,1)} async-done(((bf16[32,5120]{1,0:T(8,128)(2,1)}), bf16[128,5120]{1,0:T(8,128)(2,1)}) %all-gather.8.cloned.1.call-update) | async-done | bytes 1310736 | tf_op jit(solution)/shard_map/all_gather | solution.py:122
  152.3 3.4 fusion.70
  155.9 1.8 convolution_convert_fusion.1
  158.3 1.2 multiply_multiply_fusion.1
  159.5 28.8 %reduce-scatter.5.cloned.1.call-done = bf16[32,5120]{1,0:T(8,128)(2,1)} async-done(((bf16[128,5120]{1,0:T(8,128)(2,1)}), bf16[32,5120]{1,0:T(8,128)(2,1)}) %reduce-scatter.5.cloned.1.call-update) | async-done | bytes 327696 | tf_op jit(solution)/shard_map/reduce_scatter | solution.py:137
  188.3 1.4 broadcast_select_fusion
  190.6 3.5 collective-permute-start
  194.1 1.3 collective-permute-start.1
  195.4 5.2 collective-permute-done
  200.6 9.0 %collective-permute-done.1 = bf16[32,5120]{1,0:T(8,128)(2,1)S(1)} collective-permute-done((bf16[32,5120]{1,0:T(8,128)(2,1)S(1)}, bf16[32,5120]{1,0:T(8,128)(2,1)S(1)}, u32[]{:S(2)}, u32[]{:S(2)}) %collective-permute-start.1) | collective-permute-done | bytes 327712 | tf_op jit(solution)/shard_map/ppermute | solution.py:13
  211.4 2.1 fusion.25
  213.5 5.6 %fusion.22 = f32[3,128,5120]{2,1,0:T(8,128)} fusion(bf16[128,5120]{1,0:T(8,128)(2,1)} %all-gather.10.cloned.1.call-done, bf16[1,128,1,128]{3,1,2,0:T(8,128)(2,1)} %copy-done.19, bf16[1,128,1,128]{3,1,2,0:T(8,128)(2,1)S(1)} %fusion.91, bf16[1,128,1,128]{3,1,2,0:T(8,128)(2,1)S(1)} %fusion.90), kind=kOutput, calls=%fused_computation.32 | convolution fusion | flops 503414784 | bytes 9273344 | tf_op jit(solution)/shard_map/sd,csn->cdn/dot_general | solution.py:106
  219.2 2.4 all-gather.16.cloned.1.call-done
  221.6 3.4 fusion.55
  225.2 30.3 %all-gather.14.cloned.1.call-done = bf16[128,5120]{1,0:T(8,128)(2,1)} async-done(((bf16[32,5120]{1,0:T(8,128)(2,1)}), bf16[128,5120]{1,0:T(8,128)(2,1)}) %all-gather.14.cloned.1.call-update) | async-done | bytes 1310736 | tf_op jit(solution)/shard_map/all_gather | solution.py:73
  255.4 1.9 fusion.104
  258.7 3.5 fusion.18
  262.2 1.7 copy.28
  263.9 6.4 %fusion = bf16[3,5120,128]{1,2,0:T(8,128)(2,1)} fusion(f32[3,128,5120]{2,1,0:T(8,128)} %fusion.22, bf16[128,5120]{1,0:T(8,128)(2,1)S(1)} %copy-done.4, bf16[1,128,1,128]{3,1,2,0:T(8,128)(2,1)S(1)} %copy-done.20, bf16[1,128,1,128]{3,1,2,0:T(8,128)(2,1)S(1)} %fusion.94, bf16[1,128,1,128]{3,1,2,0:T(8,128)(2,1)S(1)} %fusion.93), kind=kOutput, calls=%fused_computation.2 | convolution fusion | flops 507346944 | bytes 13205504 | tf_op jit(solution)/shard_map/sd,csn->cdn/dot_general | solution.py:106
  270.3 6.3 %copy.23 = bf16[3,5120,128]{2,1,0:T(8,128)(2,1)} copy(bf16[3,5120,128]{1,2,0:T(8,128)(2,1)} %fusion) | data formatting | bytes 7864320 | tf_op jit(solution)/shard_map/convert_element_type | solution.py:163
  276.6 14.2 %pad_maximum_fusion = bf16[2621440]{0:T(1024)(128)(2,1)} fusion(bf16[655360]{0:T(1024)(128)(2,1)S(1)} %bitcast.314, bf16[1966080]{0:T(1024)(128)(2,1)} %bitcast.312), kind=kLoop, calls=%fused_computation.17 | loop fusion | flops 10485760 | bytes 10485760 | tf_op jit(solution)/shard_map/concatenate | solution.py:162
  290.7 2.4 fusion.3
  293.2 6.5 %collective-permute-done.2 = bf16[2621440]{0:T(1024)(128)(2,1)} collective-permute-done((bf16[2621440]{0:T(1024)(128)(2,1)}, bf16[2621440]{0:T(1024)(128)(2,1)}, u32[]{:S(2)}, u32[]{:S(2)}) %collective-permute-start.2) | collective-permute-done | bytes 5242912 | tf_op jit(solution)/shard_map/ppermute | solution.py:17
  299.7 1.5 collective-permute-start.3
  301.2 2.4 fusion.109
  303.6 20.3 %reduce-scatter.11.cloned.1.call-done = bf16[32,5120]{1,0:T(8,128)(2,1)} async-done(((bf16[128,5120]{1,0:T(8,128)(2,1)}), bf16[32,5120]{1,0:T(8,128)(2,1)}) %reduce-scatter.11.cloned.1.call-update) | async-done | bytes 327696 | tf_op jit(solution)/shard_map/reduce_scatter | solution.py:93
  323.9 1.2 fusion.122
  325.1 2.3 fusion.123
  327.8 87.3 %collective-permute-done.3 = bf16[2621440]{0:T(1024)(128)(2,1)} collective-permute-done((bf16[2621440]{0:T(1024)(128)(2,1)}, bf16[2621440]{0:T(1024)(128)(2,1)}, u32[]{:S(2)}, u32[]{:S(2)}) %collective-permute-start.3) | collective-permute-done | bytes 5242912 | tf_op jit(solution)/shard_map/ppermute | solution.py:17
  415.1 1.5 collective-permute-start.4
  416.6 3.4 fusion.60
  420.2 1.8 convolution_convert_fusion
  422.9 1.9 maximum_bitcast_fusion.1
  424.8 26.9 %reduce-scatter.9.cloned.1.call-done = bf16[32,5120]{1,0:T(8,128)(2,1)} async-done(((bf16[128,5120]{1,0:T(8,128)(2,1)}), bf16[32,5120]{1,0:T(8,128)(2,1)}) %reduce-scatter.9.cloned.1.call-update) | async-done | bytes 327696 | tf_op jit(solution)/shard_map/reduce_scatter | solution.py:137
  453.8 75.9 %collective-permute-done.4 = bf16[2621440]{0:T(1024)(128)(2,1)} collective-permute-done((bf16[2621440]{0:T(1024)(128)(2,1)}, bf16[2621440]{0:T(1024)(128)(2,1)}, u32[]{:S(2)}, u32[]{:S(2)}) %collective-permute-start.4) | collective-permute-done | bytes 5242912 | tf_op jit(solution)/shard_map/ppermute | solution.py:17
  529.7 13.3 %add_convert_fusion = bf16[2621440]{0:T(1024)(128)(2,1)S(1)} fusion(bf16[2621440]{0:T(1024)(128)(2,1)} %collective-permute-done.4, bf16[655360]{0:T(1024)(128)(2,1)S(1)} %bitcast.315, bf16[1966080]{0:T(1024)(128)(2,1)} %bitcast.313), kind=kLoop, calls=%fused_computation | loop fusion | flops 18350080 | bytes 15728640 | tf_op jit(solution)/shard_map/convert_element_type | solution.py:169
  543.1 2.1 slice.133
  545.2 1.4 slice.120
  (113 shorter events, 14.3 us)
Async XLA Ops:
  7.2 72.5 %copy-start = (bf16[1,1,128,5120]{3,2,1,0:T(8,128)(2,1)S(1)}, bf16[1,1,128,5120]{3,2,1,0:T(8,128)(2,1)}, u32[]{:S(2)}) copy-start(bf16[1,1,128,5120]{3,2,1,0:T(8,128)(2,1)} %param.17) | copy-start | bytes 3932164
  7.2 3.3 copy-start.13
  7.2 3.3 copy-start.16
  7.2 4.2 copy-start.21
  7.2 38.6 %all-gather.10.cloned.1.call-start = ((), (), s32[]{:S(2)}) async-start(), calls=%async_computation.6 | async-start | bytes 1638400 | tf_op jit(solution)/shard_map/all_gather | solution.py:72
  8.5 2.8 copy-start.23
  10.5 69.3 %all-gather.18.cloned.1.call-start = ((), (), s32[]{:S(2)}) async-start(), calls=%async_computation.13 | async-start | bytes 1638400 | tf_op jit(solution)/shard_map/all_gather | solution.py:73
  11.3 106.1 %reduce-scatter.7.cloned.1.call-start = ((), (), s32[]{:S(2)}) async-start(), calls=%async_computation.7 | async-start | bytes 1638400 | tf_op jit(solution)/shard_map/reduce_scatter | solution.py:93
  81.7 0.6 copy-start.19
  86.8 0.7 copy-start.22
  86.8 1.2 copy-start.15
  86.9 30.6 %copy-start.2 = (bf16[1,1,2,32,5120]{4,3,2,1,0:T(8,128)(2,1)S(1)}, bf16[1,1,2,32,5120]{4,3,2,1,0:T(8,128)(2,1)}, u32[]{:S(2)}) copy-start(bf16[1,1,2,32,5120]{4,3,2,1,0:T(8,128)(2,1)} %param.20) | copy-start | bytes 1966084
  86.9 30.6 %copy-start.12 = (f32[1,1,5120]{2,1,0:T(1,128)S(1)}, f32[1,1,5120]{2,1,0:T(1,128)}, u32[]{:S(2)}) copy-start(f32[1,1,5120]{2,1,0:T(1,128)} %param.15) | copy-start | bytes 61444
  86.9 65.4 %all-gather.8.cloned.1.call-start = ((), (), s32[]{:S(2)}) async-start(), calls=%async_computation.4 | async-start | bytes 1638400 | tf_op jit(solution)/shard_map/all_gather | solution.py:122
  121.0 67.4 %reduce-scatter.5.cloned.1.call-start = ((), (), s32[]{:S(2)}) async-start(), calls=%async_computation.5 | async-start | bytes 1638400 | tf_op jit(solution)/shard_map/reduce_scatter | solution.py:137
  157.7 0.6 copy-start.24
  157.7 30.6 %copy-start.10 = (bf16[1,1,32,5120]{3,2,1,0:T(8,128)(2,1)S(1)}, bf16[1,1,32,5120]{3,2,1,0:T(8,128)(2,1)}, u32[]{:S(2)}) copy-start(bf16[1,1,32,5120]{3,2,1,0:T(8,128)(2,1)} %slice_select_fusion) | copy-start | bytes 983044
  157.7 30.6 %copy-start.11 = (bf16[32,5120]{1,0:T(8,128)(2,1)S(1)}, bf16[32,5120]{1,0:T(8,128)(2,1)}, u32[]{:S(2)}) copy-start(bf16[32,5120]{1,0:T(8,128)(2,1)} %reduce-scatter.7.cloned.1.call-done) | copy-start | bytes 983044
  157.7 63.9 %all-gather.16.cloned.1.call-start = ((), (), s32[]{:S(2)}) async-start(), calls=%async_computation.11 | async-start | bytes 1638400 | tf_op jit(solution)/shard_map/all_gather | solution.py:72
  159.5 95.9 %all-gather.14.cloned.1.call-start = ((), (), s32[]{:S(2)}) async-start(), calls=%async_computation.10 | async-start | bytes 1638400 | tf_op jit(solution)/shard_map/all_gather | solution.py:73
  188.3 22.0 %copy-start.14 = (bf16[1,2,32,5120]{3,2,1,0:T(8,128)(2,1)S(1)}, bf16[1,2,32,5120]{3,2,1,0:T(8,128)(2,1)}, u32[]{:S(2)}) copy-start(bf16[1,2,32,5120]{3,2,1,0:T(8,128)(2,1)} %param.21) | copy-start | bytes 1966084
  189.7 0.7 copy-start.6
  189.7 0.9 copy-start.8
  190.4 20.9 %copy-start.3 = (bf16[1,1,128,5120]{3,2,1,0:T(8,128)(2,1)S(1)}, bf16[1,1,128,5120]{3,2,1,0:T(8,128)(2,1)}, u32[]{:S(2)}) copy-start(bf16[1,1,128,5120]{3,2,1,0:T(8,128)(2,1)} %all-gather.18.cloned.1.call-done) | copy-start | bytes 3932164
  190.6 10.1 %collective-permute-start = (bf16[32,5120]{1,0:T(8,128)(2,1)S(1)}, bf16[32,5120]{1,0:T(8,128)(2,1)S(1)}, u32[]{:S(2)}, u32[]{:S(2)}) collective-permute-start(bf16[32,5120]{1,0:T(8,128)(2,1)S(1)} %broadcast_select_fusion.1), channel_id=1, source_target_pairs={{0,8},{8,16},{16,24},{1,9},{9,17},{17,25},{2,10},{10,18},{18,26},{... | collective-permute-start | bytes 983048 | tf_op jit(solution)/shard_map/ppermute | solution.py:13
  194.1 15.5 %collective-permute-start.1 = (bf16[32,5120]{1,0:T(8,128)(2,1)S(1)}, bf16[32,5120]{1,0:T(8,128)(2,1)S(1)}, u32[]{:S(2)}, u32[]{:S(2)}) collective-permute-start(bf16[32,5120]{1,0:T(8,128)(2,1)S(1)} %get-tuple-element.6), channel_id=1, source_target_pairs={{8,0},{16,8},{24,16},{9,1},{17,9},{25,17},{10,2},{18,10},{26,18},{... | collective-permute-start | bytes 983048 | tf_op jit(solution)/shard_map/ppermute | solution.py:13
  200.6 9.0 %copy-start.17 = (bf16[32,5120]{1,0:T(8,128)(2,1)}, bf16[32,5120]{1,0:T(8,128)(2,1)S(1)}, u32[]{:S(2)}) copy-start(bf16[32,5120]{1,0:T(8,128)(2,1)S(1)} %collective-permute-done) | copy-start | bytes 983044
  209.6 0.7 copy-start.18
  211.1 112.8 %reduce-scatter.11.cloned.1.call-start = ((), (), s32[]{:S(2)}) async-start(), calls=%async_computation.12 | async-start | bytes 1638400 | tf_op jit(solution)/shard_map/reduce_scatter | solution.py:93
  255.4 3.3 copy-start.5
  262.2 1.7 copy-start.4
  262.2 1.7 copy-start.20
  276.6 14.2 %copy-start.1 = (bf16[1,1,3,5120,128]{4,3,2,1,0:T(8,128)(2,1)S(1)}, bf16[1,1,3,5120,128]{4,3,2,1,0:T(8,128)(2,1)}, u32[]{:S(2)}) copy-start(bf16[1,1,3,5120,128]{4,3,2,1,0:T(8,128)(2,1)} %param.16) | copy-start | bytes 11796484
  290.7 9.0 %collective-permute-start.2 = (bf16[2621440]{0:T(1024)(128)(2,1)}, bf16[2621440]{0:T(1024)(128)(2,1)}, u32[]{:S(2)}, u32[]{:S(2)}) collective-permute-start(bf16[2621440]{0:T(1024)(128)(2,1)} %pad_maximum_fusion), channel_id=1, source_target_pairs={{0,1},{1,0},{8,9},{9,8},{16,17},{17,16},{24,25},{25,24},{2,3},{3,2... | collective-permute-start | bytes 15728648 | tf_op jit(solution)/shard_map/ppermute | solution.py:17
  293.1 8.1 %copy-start.25 = (s32[32]{0:T(128)S(1)}, s32[32]{0:T(128)}, u32[]{:S(2)}) copy-start(s32[32]{0:T(128)} %get-tuple-element.19) | copy-start | bytes 388
  293.1 123.4 %all-gather.12.cloned.1.call-start = ((), (), s32[]{:S(2)}) async-start(), calls=%async_computation.8 | async-start | bytes 1638400 | tf_op jit(solution)/shard_map/all_gather | solution.py:122
  299.7 115.4 %collective-permute-start.3 = (bf16[2621440]{0:T(1024)(128)(2,1)}, bf16[2621440]{0:T(1024)(128)(2,1)}, u32[]{:S(2)}, u32[]{:S(2)}) collective-permute-start(bf16[2621440]{0:T(1024)(128)(2,1)} %collective-permute-done.2), channel_id=1, source_target_pairs={{0,8},{1,9},{8,0},{9,1},{16,24},{17,25},{24,16},{25,17},{2,10},{3,... | collective-permute-start | bytes 15728648 | tf_op jit(solution)/shard_map/ppermute | solution.py:17
  327.5 92.5 %copy-start.26 = (s32[128]{0:T(128)S(1)}, s32[128]{0:T(128)}, u32[]{:S(2)}) copy-start(s32[128]{0:T(128)} %get-tuple-element.17) | copy-start | bytes 1540
  327.5 124.2 %reduce-scatter.9.cloned.1.call-start = ((), (), s32[]{:S(2)}) async-start(), calls=%async_computation.9 | async-start | bytes 1638400 | tf_op jit(solution)/shard_map/reduce_scatter | solution.py:137
  415.1 114.5 %collective-permute-start.4 = (bf16[2621440]{0:T(1024)(128)(2,1)}, bf16[2621440]{0:T(1024)(128)(2,1)}, u32[]{:S(2)}, u32[]{:S(2)}) collective-permute-start(bf16[2621440]{0:T(1024)(128)(2,1)} %collective-permute-done.3), channel_id=1, source_target_pairs={{0,16},{1,17},{8,24},{9,25},{16,0},{17,1},{24,8},{25,9},{2,18},{3,... | collective-permute-start | bytes 15728648 | tf_op jit(solution)/shard_map/ppermute | solution.py:17
  422.0 1.0 copy-start.9
  422.0 30.9 %copy-start.7 = (bf16[32,5120]{1,0:T(8,128)(2,1)S(1)}, bf16[32,5120]{1,0:T(8,128)(2,1)}, u32[]{:S(2)}) copy-start(bf16[32,5120]{1,0:T(8,128)(2,1)} %copy-done.6) | copy-start | bytes 983044
Sparse Core Ops, SparseCore 0:
  10.6 35.2 all-gather.9
  48.0 31.6 all-gather.17
  87.0 30.4 reduce-scatter.6
  121.1 31.1 all-gather.7
  157.8 30.4 reduce-scatter.4
  190.3 31.1 all-gather.15
  223.7 31.6 all-gather.13
  293.3 30.6 reduce-scatter.10
  327.6 31.1 all-gather.11
  422.1 29.5 reduce-scatter.8
where the time goes:
time: 554 us; the launch traced here: 553 us
  waiting for transfers between devices  416 us (75%)
  matrix products  52.3 us (9%)
  other arithmetic  46.1 us (8%)
  local copies, waits for them, and re-layouts  16.3 us (3%)
  between operations  14.5 us (3%)
  starting transfers between devices  8.56 us (2%)
    ppermute x3, waiting for transfers between devices, swapped(): lax.ppermute(value, axis, [(i, i ^ 1 << apart) for i in range(lax.axis_si...  170 us
    all_gather x2, waiting for transfers between devices, backward_layer(): lax.all_gather(upstream, 'tp', axis=0, tiled=True)  60.5 us
    reduce_scatter x2, waiting for transfers between devices, shards(): lax.psum_scatter(jnp.dot(forward_mixed, out_weight, preferred_element_typ...  55.7 us
    reduce_scatter x2, waiting for transfers between devices, backward_layer(): lax.psum_scatter(jnp.einsum('csn,cdn->sd', d_projected, qkv_weight, prefe...  47.7 us
    all_gather x2, waiting for transfers between devices, backward_layer(): lax.all_gather(normed, 'tp', axis=0, tiled=True)  36.8 us
    all_gather x2, waiting for transfers between devices, shards(): lax.all_gather(forward_normed, 'tp', axis=0, tiled=True)  30.7 us
    ppermute x2, waiting for transfers between devices, passed_along(): return lax.ppermute(block, axis, route)  14.2 us
    concatenate x1, other arithmetic, shards(): jnp.concatenate([qkv_total.astype(jnp.bfloat16).reshape(-1), out_total.as...  14.2 us
  transfers between devices with their start and end apart: 15, of which 14 were waited for; matrix products, arithmetic and copies ran while one was open for 7% of the time, Pallas kernels for 0%

commit v1 on v0

--- a/solution.py
+++ b/solution.py
@@ -5,6 +5,20 @@
 from jax.sharding import PartitionSpec as P
 
 HD = 128
+
+
+def work_both_ways(shard, axis, dim, make, out_dim):
+    ways, here, step = (lax.axis_size(axis), lax.axis_index(axis), shard.shape[dim])
+    earlier, later = ([], [])
+    going_up = going_down = shard
+    for far in range(ways // 2 + 1):
+        earlier.append(make(going_up, (here - far) % ways * step))
+        if 0 < far < ways - ways // 2:
+            later.append(make(going_down, (here + far) % ways * step))
+        going_up = lax.ppermute(going_up, axis, [(d, (d + 1) % ways) for d in range(ways)])
+        going_down = lax.ppermute(going_down, axis, [(d, (d - 1) % ways) for d in range(ways)])
+    line = jnp.concatenate([*earlier[::-1], *later], axis=out_dim)
+    return jnp.roll(line, (here - ways // 2) * earlier[0].shape[out_dim], axis=out_dim)
 
 
 def passed_along(block, axis, distance):
@@ -119,9 +133,14 @@
         embedded = embedding(feats[0, step_index], types[0, step_index], type_table)
         current = jnp.where(position == 0, embedded, forward_in)
         forward_normed = normalize(current.astype(jnp.float32), gain_row).astype(jnp.bfloat16)
-        forward_normed_full = lax.all_gather(forward_normed, "tp", axis=0, tiled=True)
-        forward_projected = jnp.einsum(
-            "sd,cdn->csn", forward_normed_full, qkv_weight, preferred_element_type=jnp.float32
+        forward_projected = work_both_ways(
+            forward_normed,
+            "tp",
+            0,
+            lambda part, at: jnp.einsum(
+                "sd,cdn->csn", part, qkv_weight, preferred_element_type=jnp.float32
+            ),
+            1,
         ).astype(jnp.bfloat16)
         forward_heads_view = forward_projected.reshape(3, seq_len, heads_here, HD)
         forward_mixed = (

time: 554 us -> 548 us (0.989)
  waiting for transfers between devices: 416 us -> 400 us
    ppermute x0 -> x6, waiting for transfers between devices: none -> 32.8 us  [the longest x4 32.8 us: work_both_ways(): lax.ppermute(going_up, axis, [(d, (d + 1) % ways) for d in range(ways)])]
    all_gather x2 -> x0, waiting for transfers between devices: 30.7 us -> none  [shards(): lax.all_gather(forward_normed, 'tp', axis=0, tiled=True)]
    ppermute x3, waiting for transfers between devices: 170 us -> 146 us  [swapped(): lax.ppermute(value, axis, [(i, i ^ 1 << apart) for i in range(lax.axis_si...]
    reduce_scatter x2, waiting for transfers between devices: 47.7 us -> 55.1 us  [backward_layer(): lax.psum_scatter(jnp.einsum('csn,cdn->sd', d_projected, qkv_weight, prefe...]
  transfers between devices with their start and end apart: 15 -> 19, of which waited for: 14 -> 16; matrix products, arithmetic and copies ran while one was open for 7% -> 9% of each run, Pallas kernels for 0% -> 0%
where the time goes in v1:
time: 548 us; the launch traced here: 547 us
  waiting for transfers between devices  400 us (73%)
  matrix products  56.6 us (10%)
  other arithmetic  45.7 us (8%)
  local copies, waits for them, and re-layouts  17.2 us (3%)
  between operations  14.6 us (3%)
  starting transfers between devices  13.3 us (2%)
    ppermute x3, waiting for transfers between devices, swapped(): lax.ppermute(value, axis, [(i, i ^ 1 << apart) for i in range(lax.axis_si...  146 us
    all_gather x2, waiting for transfers between devices, backward_layer(): lax.all_gather(upstream, 'tp', axis=0, tiled=True)  60.3 us
    reduce_scatter x2, waiting for transfers between devices, shards(): lax.psum_scatter(jnp.dot(forward_mixed, out_weight, preferred_element_typ...  56.7 us
    reduce_scatter x2, waiting for transfers between devices, backward_layer(): lax.psum_scatter(jnp.einsum('csn,cdn->sd', d_projected, qkv_weight, prefe...  55.1 us
    all_gather x2, waiting for transfers between devices, backward_layer(): lax.all_gather(normed, 'tp', axis=0, tiled=True)  34.5 us
    ppermute x4, waiting for transfers between devices, work_both_ways(): lax.ppermute(going_up, axis, [(d, (d + 1) % ways) for d in range(ways)])  32.8 us
    ppermute x2, waiting for transfers between devices, passed_along(): return lax.ppermute(block, axis, route)  14.2 us
    convert_element_type x1, other arithmetic, shards(): (own_terms.astype(jnp.float32) + partner.astype(jnp.float32)).astype(jnp....  13.3 us
  transfers between devices with their start and end apart: 19, of which 16 were waited for; matrix products, arithmetic and copies ran while one was open for 9% of the time, Pallas kernels for 0%

profile of v1, /device:TPU:0, one launch (start us, length us, event | category | flops | bytes accessed | tf_op | source)
XLA Modules:
  0.0 547.4 jit_solution(11840816411865450984)
XLA Ops:
  9.0 1.9 fusion.131
  11.0 1.8 slice_select_fusion
  13.7 32.6 %all-gather.6.cloned.1.call-done = bf16[128,5120]{1,0:T(8,128)(2,1)} async-done(((bf16[32,5120]{1,0:T(8,128)(2,1)}), bf16[128,5120]{1,0:T(8,128)(2,1)}) %all-gather.6.cloned.1.call-update) | async-done | bytes 1310736 | tf_op jit(solution)/shard_map/all_gather | solution.py:86
  46.3 3.4 fusion.60
  49.9 30.3 %all-gather.12.cloned.1.call-done = bf16[1,1,128,5120]{3,2,1,0:T(8,128)(2,1)} async-done(((bf16[1,1,32,5120]{3,2,1,0:T(8,128)(2,1)}), bf16[1,1,128,5120]{3,2,1,0:T(8,128)(2,1)}) %all-gather.12.cloned.1.call-update) | async-done | bytes 1310736 | tf_op jit(solution)/shard_map/all_gather | solution.py:87
  80.2 1.8 fusion.113
  82.8 4.6 fusion.2
  88.6 1.5 multiply_reduce_fusion
  90.1 27.9 %reduce-scatter.7.cloned.1.call-done = bf16[32,5120]{1,0:T(8,128)(2,1)} async-done(((bf16[128,5120]{1,0:T(8,128)(2,1)}), bf16[32,5120]{1,0:T(8,128)(2,1)}) %reduce-scatter.7.cloned.1.call-update) | async-done | bytes 327696 | tf_op jit(solution)/shard_map/reduce_scatter | solution.py:107
  118.0 1.9 fusion.133
  123.4 2.8 fusion.75
  126.2 12.2 %collective-permute-done = bf16[32,5120]{1,0:T(8,128)(2,1)S(1)} collective-permute-done((bf16[32,5120]{1,0:T(8,128)(2,1)S(1)}, bf16[32,5120]{1,0:T(8,128)(2,1)S(1)}, u32[]{:S(2)}, u32[]{:S(2)}) %collective-permute-start) | collective-permute-done | bytes 327712 | tf_op jit(solution)/shard_map/ppermute | solution.py:18
  140.2 8.5 %collective-permute-done.1 = bf16[32,5120]{1,0:T(8,128)(2,1)S(1)} collective-permute-done((bf16[32,5120]{1,0:T(8,128)(2,1)S(1)}, bf16[32,5120]{1,0:T(8,128)(2,1)S(1)}, u32[]{:S(2)}, u32[]{:S(2)}) %collective-permute-start.1) | collective-permute-done | bytes 327712 | tf_op jit(solution)/shard_map/ppermute | solution.py:18
  151.3 2.6 convolution_convert_fusion.1
  154.7 28.8 %reduce-scatter.5.cloned.1.call-done = bf16[32,5120]{1,0:T(8,128)(2,1)} async-done(((bf16[128,5120]{1,0:T(8,128)(2,1)}), bf16[32,5120]{1,0:T(8,128)(2,1)}) %reduce-scatter.5.cloned.1.call-update) | async-done | bytes 327696 | tf_op jit(solution)/shard_map/reduce_scatter | solution.py:156
  183.6 1.4 broadcast_select_fusion
  185.8 3.4 collective-permute-start.3
  190.5 5.2 collective-permute-done.3
  195.7 8.9 %collective-permute-done.4 = bf16[32,5120]{1,0:T(8,128)(2,1)S(1)} collective-permute-done((bf16[32,5120]{1,0:T(8,128)(2,1)S(1)}, bf16[32,5120]{1,0:T(8,128)(2,1)S(1)}, u32[]{:S(2)}, u32[]{:S(2)}) %collective-permute-start.4) | collective-permute-done | bytes 327712 | tf_op jit(solution)/shard_map/ppermute | solution.py:27
  206.4 3.5 fusion.36
  209.9 5.0 fusion.33
  214.9 1.9 all-gather.10.cloned.1.call-done
  216.8 3.4 fusion.55
  220.4 30.1 %all-gather.8.cloned.1.call-done = bf16[128,5120]{1,0:T(8,128)(2,1)} async-done(((bf16[32,5120]{1,0:T(8,128)(2,1)}), bf16[128,5120]{1,0:T(8,128)(2,1)}) %all-gather.8.cloned.1.call-update) | async-done | bytes 1310736 | tf_op jit(solution)/shard_map/all_gather | solution.py:87
  250.5 1.9 fusion.118
  253.8 3.5 fusion.30
  257.2 1.6 copy.28
  258.8 6.8 %fusion = bf16[3,5120,128]{1,2,0:T(8,128)(2,1)} fusion(f32[3,128,5120]{2,1,0:T(8,128)} %fusion.33, bf16[128,5120]{1,0:T(8,128)(2,1)} %all-gather.10.cloned.1.call-done, bf16[1,128,1,128]{3,1,2,0:T(8,128)(2,1)} %fusion.112, bf16[1,128,1,128]{3,1,2,0:T(8,128)(2,1)S(1)} %fusion.108, bf16[1,128,1,128]{3,1,2,0:T(8,128)(2,1)S(1)} %fusion.107), kind=kOutput, calls=%fused_computation.2 | convolution fusion | flops 507346944 | bytes 13205504 | tf_op jit(solution)/shard_map/sd,csn->cdn/dot_general | solution.py:120
  265.6 6.3 %copy.23 = bf16[3,5120,128]{2,1,0:T(8,128)(2,1)} copy(bf16[3,5120,128]{1,2,0:T(8,128)(2,1)} %fusion) | data formatting | bytes 7864320 | tf_op jit(solution)/shard_map/convert_element_type | solution.py:182
  271.9 13.0 %pad_maximum_fusion = bf16[2621440]{0:T(1024)(128)(2,1)S(1)} fusion(bf16[655360]{0:T(1024)(128)(2,1)S(1)} %bitcast.356, bf16[1966080]{0:T(1024)(128)(2,1)} %bitcast.354), kind=kLoop, calls=%fused_computation.17 | loop fusion | flops 10485760 | bytes 10485760 | tf_op jit(solution)/shard_map/concatenate | solution.py:181
  284.9 8.8 %collective-permute-done.8 = bf16[2621440]{0:T(1024)(128)(2,1)} collective-permute-done((bf16[2621440]{0:T(1024)(128)(2,1)S(1)}, bf16[2621440]{0:T(1024)(128)(2,1)}, u32[]{:S(2)}, u32[]{:S(2)}) %collective-permute-start.8) | collective-permute-done | bytes 5242912 | tf_op jit(solution)/shard_map/ppermute | solution.py:31
  293.7 1.5 collective-permute-start.9
  295.2 2.4 fusion.3
  297.7 2.5 fusion.123
  300.1 27.2 %reduce-scatter.11.cloned.1.call-done = bf16[32,5120]{1,0:T(8,128)(2,1)} async-done(((bf16[128,5120]{1,0:T(8,128)(2,1)}), bf16[32,5120]{1,0:T(8,128)(2,1)}) %reduce-scatter.11.cloned.1.call-update) | async-done | bytes 327696 | tf_op jit(solution)/shard_map/reduce_scatter | solution.py:107
  327.3 1.3 fusion.136
  328.7 2.2 fusion.137
  332.9 2.8 fusion.87
  335.7 12.2 %collective-permute-done.5 = bf16[32,5120]{1,0:T(8,128)(2,1)S(1)} collective-permute-done((bf16[32,5120]{1,0:T(8,128)(2,1)S(1)}, bf16[32,5120]{1,0:T(8,128)(2,1)S(1)}, u32[]{:S(2)}, u32[]{:S(2)}) %collective-permute-start.5) | collective-permute-done | bytes 327712 | tf_op jit(solution)/shard_map/ppermute | solution.py:18
  349.8 59.4 %collective-permute-done.9 = bf16[2621440]{0:T(1024)(128)(2,1)} collective-permute-done((bf16[2621440]{0:T(1024)(128)(2,1)}, bf16[2621440]{0:T(1024)(128)(2,1)}, u32[]{:S(2)}, u32[]{:S(2)}) %collective-permute-start.9) | collective-permute-done | bytes 5242912 | tf_op jit(solution)/shard_map/ppermute | solution.py:31
  409.1 1.5 collective-permute-start.10
  411.9 1.8 convolution_convert_fusion
  413.7 1.9 maximum_bitcast_fusion.1
  415.6 27.8 %reduce-scatter.9.cloned.1.call-done = bf16[32,5120]{1,0:T(8,128)(2,1)} async-done(((bf16[128,5120]{1,0:T(8,128)(2,1)}), bf16[32,5120]{1,0:T(8,128)(2,1)}) %reduce-scatter.9.cloned.1.call-update) | async-done | bytes 327696 | tf_op jit(solution)/shard_map/reduce_scatter | solution.py:156
  445.5 78.2 %collective-permute-done.10 = bf16[2621440]{0:T(1024)(128)(2,1)} collective-permute-done((bf16[2621440]{0:T(1024)(128)(2,1)}, bf16[2621440]{0:T(1024)(128)(2,1)}, u32[]{:S(2)}, u32[]{:S(2)}) %collective-permute-start.10) | collective-permute-done | bytes 5242912 | tf_op jit(solution)/shard_map/ppermute | solution.py:31
  523.6 13.3 %add_convert_fusion = bf16[2621440]{0:T(1024)(128)(2,1)S(1)} fusion(bf16[2621440]{0:T(1024)(128)(2,1)} %collective-permute-done.10, bf16[655360]{0:T(1024)(128)(2,1)S(1)} %bitcast.357, bf16[1966080]{0:T(1024)(128)(2,1)} %bitcast.355), kind=kLoop, calls=%fused_computation | loop fusion | flops 18350080 | bytes 15728640 | tf_op jit(solution)/shard_map/convert_element_type | solution.py:188
  537.1 2.1 slice.133
  539.2 1.4 slice.120
  (129 shorter events, 26.5 us)
Async XLA Ops:
  7.2 73.0 %copy-start = (bf16[1,1,128,5120]{3,2,1,0:T(8,128)(2,1)S(1)}, bf16[1,1,128,5120]{3,2,1,0:T(8,128)(2,1)}, u32[]{:S(2)}) copy-start(bf16[1,1,128,5120]{3,2,1,0:T(8,128)(2,1)} %param.19) | copy-start | bytes 3932164
  7.2 39.1 %all-gather.6.cloned.1.call-start = ((), (), s32[]{:S(2)}) async-start(), calls=%async_computation.5 | async-start | bytes 1638400 | tf_op jit(solution)/shard_map/all_gather | solution.py:86
  8.5 0.6 copy-start.25
  10.9 69.3 %all-gather.12.cloned.1.call-start = ((), (), s32[]{:S(2)}) async-start(), calls=%async_computation.11 | async-start | bytes 1638400 | tf_op jit(solution)/shard_map/all_gather | solution.py:87
  12.9 105.2 %reduce-scatter.7.cloned.1.call-start = ((), (), s32[]{:S(2)}) async-start(), calls=%async_computation.6 | async-start | bytes 1638400 | tf_op jit(solution)/shard_map/reduce_scatter | solution.py:107
  82.0 6.0 %copy-start.24 = (s32[1,2,32]{2,1,0:T(2,128)S(1)}, s32[1,2,32]{2,1,0:T(2,128)}, u32[]{:S(2)}) copy-start(s32[1,2,32]{2,1,0:T(2,128)} %param.14) | copy-start | bytes 772
  82.0 6.6 %copy-start.15 = (bf16[64,5120]{1,0:T(8,128)(2,1)S(1)}, bf16[64,5120]{1,0:T(8,128)(2,1)}, u32[]{:S(2)}) copy-start(bf16[64,5120]{1,0:T(8,128)(2,1)} %param.16) | copy-start | bytes 1966084
  82.2 0.6 copy-start.20
  82.8 35.2 %copy-start.4 = (bf16[1,1,2,32,5120]{4,3,2,1,0:T(8,128)(2,1)S(1)}, bf16[1,1,2,32,5120]{4,3,2,1,0:T(8,128)(2,1)}, u32[]{:S(2)}) copy-start(bf16[1,1,2,32,5120]{4,3,2,1,0:T(8,128)(2,1)} %param.22) | copy-start | bytes 1966084
  82.8 35.2 %copy-start.13 = (f32[1,1,5120]{2,1,0:T(1,128)S(1)}, f32[1,1,5120]{2,1,0:T(1,128)}, u32[]{:S(2)}) copy-start(f32[1,1,5120]{2,1,0:T(1,128)} %param.17) | copy-start | bytes 61444
  87.4 96.1 %reduce-scatter.5.cloned.1.call-start = ((), (), s32[]{:S(2)}) async-start(), calls=%async_computation.4 | async-start | bytes 1638400 | tf_op jit(solution)/shard_map/reduce_scatter | solution.py:156
  118.0 20.8 %copy-start.1 = (bf16[1,1,3,5120,128]{4,3,2,1,0:T(8,128)(2,1)S(1)}, bf16[1,1,3,5120,128]{4,3,2,1,0:T(8,128)(2,1)}, u32[]{:S(2)}) copy-start(bf16[1,1,3,5120,128]{4,3,2,1,0:T(8,128)(2,1)} %param.18) | copy-start | bytes 11796484
  120.0 0.5 copy-start.22
  121.4 18.1 %collective-permute-start.2 = (bf16[32,5120]{1,0:T(8,128)(2,1)S(1)}, bf16[32,5120]{1,0:T(8,128)(2,1)S(1)}, u32[]{:S(2)}, u32[]{:S(2)}) collective-permute-start(bf16[32,5120]{1,0:T(8,128)(2,1)S(1)} %get-tuple-element.13), channel_id=1, source_target_pairs={{0,6},{2,0},{4,2},{6,4},{1,7},{3,1},{5,3},{7,5},{8,14},{10,8},{12,... | collective-permute-start | bytes 983048 | tf_op jit(solution)/shard_map/ppermute | solution.py:19
  122.5 15.9 %collective-permute-start = (bf16[32,5120]{1,0:T(8,128)(2,1)S(1)}, bf16[32,5120]{1,0:T(8,128)(2,1)S(1)}, u32[]{:S(2)}, u32[]{:S(2)}) collective-permute-start(bf16[32,5120]{1,0:T(8,128)(2,1)S(1)} %get-tuple-element.13), channel_id=1, source_target_pairs={{0,2},{2,4},{4,6},{6,0},{1,3},{3,5},{5,7},{7,1},{8,10},{10,12},{12... | collective-permute-start | bytes 983048 | tf_op jit(solution)/shard_map/ppermute | solution.py:18
  138.3 10.3 %collective-permute-start.1 = (bf16[32,5120]{1,0:T(8,128)(2,1)S(1)}, bf16[32,5120]{1,0:T(8,128)(2,1)S(1)}, u32[]{:S(2)}, u32[]{:S(2)}) collective-permute-start(bf16[32,5120]{1,0:T(8,128)(2,1)S(1)} %collective-permute-done), channel_id=1, source_target_pairs={{0,2},{2,4},{4,6},{6,0},{1,3},{3,5},{5,7},{7,1},{8,10},{10,12},{12... | collective-permute-start | bytes 983048 | tf_op jit(solution)/shard_map/ppermute | solution.py:18
  140.2 43.4 %copy-start.11 = (bf16[1,1,32,5120]{3,2,1,0:T(8,128)(2,1)S(1)}, bf16[1,1,32,5120]{3,2,1,0:T(8,128)(2,1)}, u32[]{:S(2)}) copy-start(bf16[1,1,32,5120]{3,2,1,0:T(8,128)(2,1)} %slice_select_fusion) | copy-start | bytes 983044
  140.2 43.4 %copy-start.12 = (bf16[32,5120]{1,0:T(8,128)(2,1)S(1)}, bf16[32,5120]{1,0:T(8,128)(2,1)}, u32[]{:S(2)}) copy-start(bf16[32,5120]{1,0:T(8,128)(2,1)} %reduce-scatter.7.cloned.1.call-done) | copy-start | bytes 983044
  149.8 0.6 copy-start.19
  150.6 0.6 copy-start.18
  153.9 62.9 %all-gather.10.cloned.1.call-start = ((), (), s32[]{:S(2)}) async-start(), calls=%async_computation.9 | async-start | bytes 1638400 | tf_op jit(solution)/shard_map/all_gather | solution.py:86
  154.7 95.8 %all-gather.8.cloned.1.call-start = ((), (), s32[]{:S(2)}) async-start(), calls=%async_computation.8 | async-start | bytes 1638400 | tf_op jit(solution)/shard_map/all_gather | solution.py:87
  183.6 21.8 %copy-start.14 = (bf16[1,2,32,5120]{3,2,1,0:T(8,128)(2,1)S(1)}, bf16[1,2,32,5120]{3,2,1,0:T(8,128)(2,1)}, u32[]{:S(2)}) copy-start(bf16[1,2,32,5120]{3,2,1,0:T(8,128)(2,1)} %param.23) | copy-start | bytes 1966084
  184.9 0.8 copy-start.7
  184.9 0.8 copy-start.9
  184.9 25.0 %copy-start.6 = (bf16[128,5120]{1,0:T(8,128)(2,1)S(1)}, bf16[128,5120]{1,0:T(8,128)(2,1)}, u32[]{:S(2)}) copy-start(bf16[128,5120]{1,0:T(8,128)(2,1)} %all-gather.6.cloned.1.call-done) | copy-start | bytes 3932164
  185.8 9.9 %collective-permute-start.3 = (bf16[32,5120]{1,0:T(8,128)(2,1)S(1)}, bf16[32,5120]{1,0:T(8,128)(2,1)S(1)}, u32[]{:S(2)}, u32[]{:S(2)}) collective-permute-start(bf16[32,5120]{1,0:T(8,128)(2,1)S(1)} %broadcast_select_fusion.1), channel_id=1, source_target_pairs={{0,8},{8,16},{16,24},{1,9},{9,17},{17,25},{2,10},{10,18},{18,26},{... | collective-permute-start | bytes 983048 | tf_op jit(solution)/shard_map/ppermute | solution.py:27
  189.2 15.5 %collective-permute-start.4 = (bf16[32,5120]{1,0:T(8,128)(2,1)S(1)}, bf16[32,5120]{1,0:T(8,128)(2,1)S(1)}, u32[]{:S(2)}, u32[]{:S(2)}) collective-permute-start(bf16[32,5120]{1,0:T(8,128)(2,1)S(1)} %get-tuple-element.7), channel_id=1, source_target_pairs={{8,0},{16,8},{24,16},{9,1},{17,9},{25,17},{10,2},{18,10},{26,18},{... | collective-permute-start | bytes 983048 | tf_op jit(solution)/shard_map/ppermute | solution.py:27
  195.7 8.9 %copy-start.16 = (bf16[32,5120]{1,0:T(8,128)(2,1)}, bf16[32,5120]{1,0:T(8,128)(2,1)S(1)}, u32[]{:S(2)}) copy-start(bf16[32,5120]{1,0:T(8,128)(2,1)S(1)} %collective-permute-done.3) | copy-start | bytes 983044
  204.7 0.7 copy-start.17
  206.2 121.1 %reduce-scatter.11.cloned.1.call-start = ((), (), s32[]{:S(2)}) async-start(), calls=%async_computation.10 | async-start | bytes 1638400 | tf_op jit(solution)/shard_map/reduce_scatter | solution.py:107
  250.5 3.3 copy-start.5
  271.9 23.3 %copy-start.2 = (bf16[1,1,3,5120,128]{4,3,2,1,0:T(8,128)(2,1)S(1)}, bf16[1,1,3,5120,128]{4,3,2,1,0:T(8,128)(2,1)}, u32[]{:S(2)}) copy-start(bf16[1,1,3,5120,128]{4,3,2,1,0:T(8,128)(2,1)} %param.18) | copy-start | bytes 11796484
  271.9 23.3 %copy-start.21 = (bf16[1,128,1,128]{3,1,2,0:T(8,128)(2,1)S(1)}, bf16[1,128,1,128]{3,1,2,0:T(8,128)(2,1)}, u32[]{:S(2)}) copy-start(bf16[1,128,1,128]{3,1,2,0:T(8,128)(2,1)} %fusion.112) | copy-start | bytes 98308
  284.8 12.8 %copy-start.27 = (s32[32]{0:T(128)S(1)}, s32[32]{0:T(128)}, u32[]{:S(2)}) copy-start(s32[32]{0:T(128)} %get-tuple-element.20) | copy-start | bytes 388
  284.8 43.8 %copy-start.23 = (f32[32]{0:T(128)S(1)}, f32[32]{0:T(128)}, u32[]{:S(2)}) copy-start(f32[32]{0:T(128)} %copy-done.22) | copy-start | bytes 388
  284.8 8.9 %collective-permute-start.8 = (bf16[2621440]{0:T(1024)(128)(2,1)S(1)}, bf16[2621440]{0:T(1024)(128)(2,1)}, u32[]{:S(2)}, u32[]{:S(2)}) collective-permute-start(bf16[2621440]{0:T(1024)(128)(2,1)S(1)} %pad_maximum_fusion), channel_id=1, source_target_pairs={{0,1},{1,0},{8,9},{9,8},{16,17},{17,16},{24,25},{25,24},{2,3},{3,2... | collective-permute-start | bytes 15728648 | tf_op jit(solution)/shard_map/ppermute | solution.py:31
  293.7 115.4 %collective-permute-start.9 = (bf16[2621440]{0:T(1024)(128)(2,1)}, bf16[2621440]{0:T(1024)(128)(2,1)}, u32[]{:S(2)}, u32[]{:S(2)}) collective-permute-start(bf16[2621440]{0:T(1024)(128)(2,1)} %collective-permute-done.8), channel_id=1, source_target_pairs={{0,8},{1,9},{8,0},{9,1},{16,24},{17,25},{24,16},{25,17},{2,10},{3,... | collective-permute-start | bytes 15728648 | tf_op jit(solution)/shard_map/ppermute | solution.py:31
  297.6 145.8 %reduce-scatter.9.cloned.1.call-start = ((), (), s32[]{:S(2)}) async-start(), calls=%async_computation.7 | async-start | bytes 1638400 | tf_op jit(solution)/shard_map/reduce_scatter | solution.py:156
  327.3 21.1 %copy-start.3 = (bf16[1,1,3,5120,128]{4,3,2,1,0:T(8,128)(2,1)S(1)}, bf16[1,1,3,5120,128]{4,3,2,1,0:T(8,128)(2,1)}, u32[]{:S(2)}) copy-start(bf16[1,1,3,5120,128]{4,3,2,1,0:T(8,128)(2,1)} %param.18) | copy-start | bytes 11796484
  330.9 18.2 %collective-permute-start.7 = (bf16[32,5120]{1,0:T(8,128)(2,1)S(1)}, bf16[32,5120]{1,0:T(8,128)(2,1)S(1)}, u32[]{:S(2)}, u32[]{:S(2)}) collective-permute-start(bf16[32,5120]{1,0:T(8,128)(2,1)S(1)} %get-tuple-element.11), channel_id=1, source_target_pairs={{0,6},{2,0},{4,2},{6,4},{1,7},{3,1},{5,3},{7,5},{8,14},{10,8},{12,... | collective-permute-start | bytes 983048 | tf_op jit(solution)/shard_map/ppermute | solution.py:19
  332.0 15.9 %collective-permute-start.5 = (bf16[32,5120]{1,0:T(8,128)(2,1)S(1)}, bf16[32,5120]{1,0:T(8,128)(2,1)S(1)}, u32[]{:S(2)}, u32[]{:S(2)}) collective-permute-start(bf16[32,5120]{1,0:T(8,128)(2,1)S(1)} %get-tuple-element.11), channel_id=1, source_target_pairs={{0,2},{2,4},{4,6},{6,0},{1,3},{3,5},{5,7},{7,1},{8,10},{10,12},{12... | collective-permute-start | bytes 983048 | tf_op jit(solution)/shard_map/ppermute | solution.py:18
  347.9 62.7 %collective-permute-start.6 = (bf16[32,5120]{1,0:T(8,128)(2,1)S(1)}, bf16[32,5120]{1,0:T(8,128)(2,1)S(1)}, u32[]{:S(2)}, u32[]{:S(2)}) collective-permute-start(bf16[32,5120]{1,0:T(8,128)(2,1)S(1)} %collective-permute-done.5), channel_id=1, source_target_pairs={{0,2},{2,4},{4,6},{6,0},{1,3},{3,5},{5,7},{7,1},{8,10},{10,12},{12... | collective-permute-start | bytes 983048 | tf_op jit(solution)/shard_map/ppermute | solution.py:18
  349.1 62.6 %copy-start.26 = (s32[128]{0:T(128)S(1)}, s32[128]{0:T(128)}, u32[]{:S(2)}) copy-start(s32[128]{0:T(128)} %get-tuple-element.18) | copy-start | bytes 1540
  349.7 64.0 %copy-start.10 = (bf16[32,5120]{1,0:T(8,128)(2,1)S(1)}, bf16[32,5120]{1,0:T(8,128)(2,1)}, u32[]{:S(2)}) copy-start(bf16[32,5120]{1,0:T(8,128)(2,1)} %copy-done.9) | copy-start | bytes 983044
  409.1 114.5 %collective-permute-start.10 = (bf16[2621440]{0:T(1024)(128)(2,1)}, bf16[2621440]{0:T(1024)(128)(2,1)}, u32[]{:S(2)}, u32[]{:S(2)}) collective-permute-start(bf16[2621440]{0:T(1024)(128)(2,1)} %collective-permute-done.9), channel_id=1, source_target_pairs={{0,16},{1,17},{8,24},{9,25},{16,0},{17,1},{24,8},{25,9},{2,18},{3,... | collective-permute-start | bytes 15728648 | tf_op jit(solution)/shard_map/ppermute | solution.py:31
  411.2 33.4 %copy-start.8 = (bf16[32,5120]{1,0:T(8,128)(2,1)S(1)}, bf16[32,5120]{1,0:T(8,128)(2,1)}, u32[]{:S(2)}) copy-start(bf16[32,5120]{1,0:T(8,128)(2,1)} %copy-done.7) | copy-start | bytes 983044
Sparse Core Ops, SparseCore 0:
  11.0 35.2 all-gather.5
  48.5 31.6 all-gather.11
  87.5 30.4 reduce-scatter.6
  154.0 29.4 reduce-scatter.4
  185.6 31.1 all-gather.9
  218.8 31.6 all-gather.7
  297.7 29.5 reduce-scatter.10
  413.8 29.5 reduce-scatter.8
